TPU v7x, 32 devices: a whole 2x2x4 slice. The times are simulated.
32 devices in a mesh: dp: 4 (over z), expert: 8 (over y, x, core).
Axes of the slice: x: 2, y: 2, z: 4, core: 2. Of those that a mesh axis runs over, the one named last changes fastest.
Arguments:
- hidden: bfloat16 [3072, 2880], P('expert', 'dp'), may hold values from -6 to 6
- segments: int32 [8, 384], P('expert'), may hold values from 0 to 3, never falling along the last dimension, each value on 1 to 192 neighbouring positions
- request_adapter: int32 [8, 4], P('expert'), may hold values from 0 to 7
- routes: int32 [8, 384, 4], P('expert', 'dp'), may hold values from 0 to 7, all different within a row; in each aligned block of 96 rows (0 to 95, 96 to 191, ..., all dimensions but the last counted through in order) at most 64 rows name the same one
- expert_gates: bfloat16 [8, 384, 4], P('expert', 'dp'), may hold values from 0.049804688 to 0.59765625
- attention_gain: float32 [2880], replicated, may hold values from 0.25 to 1.75
- joined_weight: bfloat16 [2880, 4, 640], P(None, 'dp'), may hold values from -0.109375 to 0.109375
- sinks: float32 [32], P('dp'), may hold values from 0 to 3
- attention_out_weight: bfloat16 [2048, 2880], P('dp'), may hold values from -0.125 to 0.125
- joined_down_maps: bfloat16 [2880, 128], replicated, may hold values from -0.109375 to 0.109375
- joined_up_maps: bfloat16 [128, 4, 640], P(None, 'dp'), may hold values from -0.375 to 0.375
- output_down_maps: bfloat16 [2048, 128], P('dp'), may hold values from -0.125 to 0.125
- output_up_maps: bfloat16 [128, 2880], P(None, 'dp'), may hold values from -0.75 to 0.75
- expert_norm_gain: float32 [2880], replicated, may hold values from 0.25 to 1.75
- expert_gate_weight: bfloat16 [8, 2880, 2880], P('expert', None, 'dp'), may hold values from -0.109375 to 0.109375
- expert_up_weight: bfloat16 [8, 2880, 2880], P('expert', None, 'dp'), may hold values from -0.109375 to 0.109375
- expert_down_weight: bfloat16 [8, 2880, 2880], P('expert', 'dp'), may hold values from -0.109375 to 0.109375
- closing_gain: float32 [2880], replicated, may hold values from 0.25 to 1.75
- vocabulary_weight: bfloat16 [2880, 25600], P(None, ('dp', 'expert')), may hold values from -0.109375 to 0.109375
Outputs:
- hidden_out: bfloat16 [3072, 2880], P('expert', 'dp')
- logits: float32 [32, 25600], P(None, ('dp', 'expert'))
Inputs may be any that keep to these rules, and one draw needn't show every extreme that they name: `segments`: in each column the ids do not fall; each of the 4 requests has 1 to 192 tokens, and one has exactly 192. `routes`: the 4 experts of a token differ. Within the rows of one device (96 consecutive tokens, aligned blocks) no expert is named more than 64 times, and in some blocks one expert is named exactly 64 times.
All inputs are finite; a program needn't handle non-finite values.
Results may differ from a plain program's by a relative error of at most 0.02.
Values may be sent and summed in bfloat16 or wider, within the bound.
No kernel may reach another device: no remote copies, remote signals or barrier semaphores. Data moves between devices by JAX's collectives and lax.ppermute only.
A program may use at most 128 MiB of HBM per device.

v0:
```python
import jax
import jax.numpy as jnp
from jax import lax
from jax.sharding import PartitionSpec as P

HEAD_SIZE = 64
QUERY_GROUP = 8
TOP = 4
ADAPTER_RANK = 16
REQS = 4
epsilon = 1e-05
theta_base = 150000.0
adapter_scale = 2.0
glu_alpha = 1.702


def rms_scale(values, gain_row):
    mean_square = jnp.mean(values * values, axis=-1, keepdims=True)
    return values * lax.rsqrt(mean_square + epsilon) * gain_row


def positions_of(segment_row):
    counter = jnp.arange(segment_row.shape[0], dtype=jnp.int32)
    starting = jnp.concatenate(
        [jnp.ones((1,), dtype=jnp.bool_), segment_row[1:] != segment_row[:-1]]
    )
    first_index = lax.cummax(jnp.where(starting, counter, 0), axis=0)
    return counter - first_index


def adapter_per_token(segment_row, adapter_row):
    hits = segment_row[:, None] == jnp.arange(adapter_row.shape[0], dtype=jnp.int32)[None, :]
    return jnp.sum(jnp.where(hits, adapter_row[None, :], 0), axis=1)


def rotate_heads(values, positions):
    head_dim = values.shape[-1]
    half_dim = head_dim // 2
    frequency = theta_base ** (-2.0 * jnp.arange(half_dim, dtype=jnp.float32) / head_dim)
    angles = positions.astype(jnp.float32)[:, None] * frequency[None, :]
    cosine = jnp.cos(angles)[:, None, :]
    sine_part = jnp.sin(angles)[:, None, :]
    first_half = values[..., :half_dim]
    second_half = values[..., half_dim:]
    return jnp.concatenate(
        [
            first_half * cosine - second_half * sine_part,
            second_half * cosine + first_half * sine_part,
        ],
        axis=-1,
    )


def attend_heads(queries, key_heads, value_heads, segment_row, sink_row):
    tokens_now, kv_now, group_now, head_dim = queries.shape
    scores = jnp.einsum(
        "tkgh,skh->kgts", queries, key_heads, preferred_element_type=jnp.float32
    ) * head_dim ** (-0.5)
    counter = jnp.arange(tokens_now, dtype=jnp.int32)
    allowed = (segment_row[:, None] == segment_row[None, :]) & (
        counter[None, :] <= counter[:, None]
    )
    weights = jnp.where(allowed[None, None], jnp.exp(scores), 0.0)
    totals = jnp.sum(weights, axis=-1, keepdims=True) + jnp.exp(sink_row).reshape(
        kv_now, group_now, 1, 1
    )
    probs = (weights / totals).astype(jnp.bfloat16)
    blended_hidden = jnp.einsum(
        "kgts,skh->tkgh", probs, value_heads, preferred_element_type=jnp.float32
    )
    return blended_hidden.astype(jnp.bfloat16).reshape(tokens_now, kv_now * group_now * head_dim)


def shards(
    hidden,
    segments,
    request_adapter,
    routes,
    expert_gates,
    attention_gain,
    joined_weight,
    sinks,
    attention_out_weight,
    joined_down_maps,
    joined_up_maps,
    output_down_maps,
    output_up_maps,
    expert_norm_gain,
    expert_gate_weight,
    expert_up_weight,
    expert_down_weight,
    closing_gain,
    vocabulary_weight,
):
    groups = lax.axis_size("dp")
    columns = lax.axis_size("expert")
    position_dp = lax.axis_index("dp")
    segment_row = segments[0]
    adapter_row = request_adapter[0]
    col_tokens = segment_row.shape[0]
    gathered_rows = lax.all_gather(hidden, "dp", axis=1, tiled=True)
    width = gathered_rows.shape[1]
    normalized_hidden = rms_scale(gathered_rows.astype(jnp.float32), attention_gain).astype(
        jnp.bfloat16
    )
    joined_projection = jnp.dot(
        normalized_hidden, joined_weight.reshape(width, -1), preferred_element_type=jnp.float32
    )
    reduced_every_adapter = joined_down_maps.shape[1]
    reduced_hidden = jnp.dot(
        normalized_hidden, joined_down_maps, preferred_element_type=jnp.float32
    ).astype(jnp.bfloat16)
    rank_owner = jnp.arange(reduced_every_adapter, dtype=jnp.int32) // ADAPTER_RANK
    adapter_mask = adapter_per_token(segment_row, adapter_row)[:, None] == rank_owner[None, :]
    selected_reduced = jnp.where(adapter_mask, reduced_hidden, jnp.zeros_like(reduced_hidden))
    joined_projection = joined_projection + adapter_scale * jnp.dot(
        selected_reduced,
        joined_up_maps.reshape(reduced_every_adapter, -1),
        preferred_element_type=jnp.float32,
    )
    kv_here = joined_weight.shape[1]
    joined_projection = joined_projection.reshape(col_tokens, kv_here, QUERY_GROUP + 2, HEAD_SIZE)
    positions = positions_of(segment_row)
    queries = rotate_heads(
        joined_projection[:, :, :QUERY_GROUP].reshape(col_tokens, kv_here * QUERY_GROUP, HEAD_SIZE),
        positions,
    )
    queries = queries.astype(jnp.bfloat16).reshape(col_tokens, kv_here, QUERY_GROUP, HEAD_SIZE)
    key_heads = rotate_heads(joined_projection[:, :, QUERY_GROUP], positions).astype(jnp.bfloat16)
    value_heads = joined_projection[:, :, QUERY_GROUP + 1].astype(jnp.bfloat16)
    blended_hidden = attend_heads(queries, key_heads, value_heads, segment_row, sinks)
    partial_out = jnp.dot(blended_hidden, attention_out_weight, preferred_element_type=jnp.float32)
    mine_out = lax.psum_scatter(
        partial_out.astype(jnp.bfloat16), "dp", scatter_dimension=1, tiled=True
    ).astype(jnp.float32)
    output_reduced = lax.psum(
        jnp.dot(blended_hidden, output_down_maps, preferred_element_type=jnp.float32).astype(
            jnp.bfloat16
        ),
        "dp",
    )
    selected_output = jnp.where(adapter_mask, output_reduced, jnp.zeros_like(output_reduced))
    adapter_delta = adapter_scale * jnp.dot(
        selected_output, output_up_maps, preferred_element_type=jnp.float32
    )
    resid = (hidden.astype(jnp.float32) + mine_out + adapter_delta).astype(jnp.bfloat16)
    share = col_tokens // groups
    column_full = lax.all_gather(resid, "dp", axis=1, tiled=True)
    own_rows = lax.dynamic_slice_in_dim(column_full, position_dp * share, share, 0)
    moe_in = rms_scale(
        lax.optimization_barrier(own_rows).astype(jnp.float32), expert_norm_gain
    ).astype(jnp.bfloat16)
    experts = expert_gate_weight.shape[0] * columns
    capacity = 4 * share * TOP // (3 * experts)
    route_flat = routes[0].reshape(-1)
    one_hot = (route_flat[:, None] == jnp.arange(experts, dtype=jnp.int32)[None, :]).astype(
        jnp.int32
    )
    slot_rows = jnp.sum((jnp.cumsum(one_hot, axis=0) - one_hot) * one_hot, axis=1)
    target = route_flat * capacity + slot_rows
    source_rows = jnp.arange(route_flat.shape[0], dtype=jnp.int32) // TOP
    table = jnp.full((experts * capacity,), share, jnp.int32).at[target].set(source_rows)
    padded = jnp.concatenate([moe_in, jnp.zeros((1, width), jnp.bfloat16)], axis=0)
    outgoing = jnp.take(padded, table, axis=0).reshape(experts, capacity, width)
    gate_weight = expert_gate_weight[0]
    up_weight = expert_up_weight[0]
    down_weight = expert_down_weight[0]
    copies = jnp.tile(outgoing, (groups, 1, 1))
    arrived = lax.all_to_all(copies, ("dp", "expert"), split_axis=0, concat_axis=0, tiled=True)
    senders = arrived.shape[0]
    slots_now = arrived.shape[1]
    rows_in = arrived.reshape(-1, width)
    gate_part = jnp.dot(rows_in, gate_weight, preferred_element_type=jnp.float32)
    up_part = jnp.dot(rows_in, up_weight, preferred_element_type=jnp.float32)
    activated = (gate_part * jax.nn.sigmoid(glu_alpha * gate_part) * (up_part + 1.0)).astype(
        jnp.bfloat16
    )
    shares_out = (
        jnp.dot(activated, down_weight, preferred_element_type=jnp.float32)
        .astype(jnp.bfloat16)
        .reshape(senders, slots_now, width)
    )
    answers = lax.all_to_all(shares_out, ("dp", "expert"), split_axis=0, concat_axis=0, tiled=True)
    merged = jnp.sum(
        answers.reshape(groups, columns, capacity, width).astype(jnp.float32), axis=0
    ).astype(jnp.bfloat16)
    picked_out = jnp.take(merged.reshape(experts * capacity, width), target, axis=0).reshape(
        share, TOP, width
    )
    mixture = jnp.einsum(
        "tk,tkd->td", expert_gates[0], picked_out, preferred_element_type=jnp.float32
    )
    moe_rounded = lax.optimization_barrier(mixture.astype(jnp.bfloat16))
    finished = (own_rows.astype(jnp.float32) + moe_rounded.astype(jnp.float32)).astype(jnp.bfloat16)
    hidden_out = lax.all_to_all(finished, "dp", split_axis=1, concat_axis=0, tiled=True)
    counter = jnp.arange(col_tokens, dtype=jnp.int32)
    request_ids = jnp.arange(REQS, dtype=jnp.int32)
    last_index = jnp.max(
        jnp.where(segment_row[None, :] == request_ids[:, None], counter[None, :], -1), axis=1
    )
    local_index = last_index - position_dp * share
    inside = (local_index >= 0) & (local_index < share)
    chosen = jnp.take(finished, jnp.clip(local_index, 0, share - 1), axis=0)
    chosen = jnp.where(inside[:, None], chosen, jnp.zeros_like(chosen))
    ends = rms_scale(chosen.astype(jnp.float32), closing_gain).astype(jnp.bfloat16)
    spread_rows = lax.all_gather(ends, ("dp", "expert"), axis=0, tiled=True)
    tail_rows = jnp.sum(
        spread_rows.reshape(groups, columns * REQS, width).astype(jnp.float32), axis=0
    ).astype(jnp.bfloat16)
    logits = jnp.dot(tail_rows, vocabulary_weight, preferred_element_type=jnp.float32)
    return (hidden_out, logits)


def solution(mesh):
    in_specs = (
        P("expert", "dp"),
        P("expert", None),
        P("expert", None),
        P("expert", "dp", None),
        P("expert", "dp", None),
        P(),
        P(None, "dp", None),
        P("dp"),
        P("dp", None),
        P(),
        P(None, "dp", None),
        P("dp", None),
        P(None, "dp"),
        P(),
        P("expert", None, "dp"),
        P("expert", None, "dp"),
        P("expert", "dp", None),
        P(),
        P(None, ("dp", "expert")),
    )
    out_specs = (P("expert", "dp"), P(None, ("dp", "expert")))
    return jax.shard_map(shards, mesh=mesh, in_specs=in_specs, out_specs=out_specs, check_vma=False)
```

profile of v0, /device:TPU:0, one launch (start us, length us, event | category | flops | bytes accessed | tf_op | source)
XLA Modules:
  0.0 916.7 jit_solution(5084641404369946867)
XLA Ops:
  12.1 48.3 %all-gather.4.cloned.1.call-done = bf16[384,2880]{0,1:T(8,128)(2,1)} async-done(((bf16[384,720]{0,1:T(8,128)(2,1)}), bf16[384,2880]{0,1:T(8,128)(2,1)}) %all-gather.4.cloned.1.call-update) | async-done | bytes 2211856 | tf_op jit(solution)/shard_map/all_gather | solution.py:101
  62.6 5.9 fusion.11
  68.5 4.8 fusion.21
  73.3 2.5 copy.59
  83.7 4.1 convolution_convert_fusion.1
  87.9 29.0 %all-reduce.3.cloned.1.call-done = bf16[384,128]{1,0:T(8,128)(2,1)} async-done(((bf16[384,128]{1,0:T(8,128)(2,1)}), bf16[384,128]{1,0:T(8,128)(2,1)}) %all-reduce.3.cloned.1.call-update) | async-done | bytes 98320 | tf_op jit(solution)/shard_map/psum | solution.py:136
  116.8 48.0 %reduce-scatter.2.cloned.1.call-done = bf16[384,720]{0,1:T(8,128)(2,1)} async-done(((bf16[384,2880]{0,1:T(8,128)(2,1)}), bf16[384,720]{0,1:T(8,128)(2,1)}) %reduce-scatter.2.cloned.1.call-update) | async-done | bytes 552976 | tf_op jit(solution)/shard_map/reduce_scatter | solution.py:133
  169.2 3.1 scatter_custom_fusion
  172.4 42.6 %all-gather.6.cloned.1.call-done = bf16[384,2880]{0,1:T(8,128)(2,1)} async-done(((bf16[384,720]{0,1:T(8,128)(2,1)}), bf16[384,2880]{0,1:T(8,128)(2,1)}) %all-gather.6.cloned.1.call-update) | async-done | bytes 2211856 | tf_op jit(solution)/shard_map/all_gather | solution.py:148
  217.9 3.7 gather_fusion
  223.8 6.0 tile.8
  229.8 266.5 %all_to_all.29 = bf16[32,64,2880]{2,1,0:T(8,128)(2,1)} all-to-all(bf16[32,64,2880]{2,1,0:T(8,128)(2,1)} %bitcast.115), channel_id=1, replica_groups=mesh['dp'=4,'expert'=8] {'dp','expert'}, dimensions={0} | all-to-all | bytes 23592960 | tf_op jit(solution)/shard_map/all_to_all | solution.py:169
  496.3 15.1 %fusion.4 = f32[2048,720]{0,1:T(8,128)} fusion(bf16[2048,2880]{1,0:T(8,128)(2,1)} %bitcast.26, bf16[1,2880,720]{1,2,0:T(8,128)(2,1)} %param.34), kind=kOutput, calls=%fused_computation.15 | convolution fusion | flops 8493465600 | bytes 21841920 | tf_op jit(solution)/shard_map/dot_general | solution.py:174
  511.4 26.6 %convolution_convert_fusion = bf16[2048,2880]{0,1:T(8,128)(2,1)} fusion(bf16[1,720,2880]{2,1,0:T(8,128)(2,1)} %param.35, f32[2048,720]{0,1:T(8,128)} %fusion.4, bf16[2048,2880]{1,0:T(8,128)(2,1)} %bitcast.26, bf16[1,2880,720]{1,2,0:T(8,128)(2,1)} %param.33), kind=kOutput, calls=%fused_computation.4 | convolution fusion | flops 17004625920 | bytes 37785600 | tf_op jit(solution)/shard_map/dot_general | solution.py:179
  538.0 16.3 %copy.67 = bf16[2048,2880]{1,0:T(8,128)(2,1)} copy(bf16[2048,2880]{0,1:T(8,128)(2,1)} %convolution_convert_fusion) | data formatting | bytes 23592960 | tf_op jit(solution)/shard_map/convert_element_type | solution.py:180
  554.4 4.1 all-to-all-start.1
  559.1 266.6 %all-to-all-done.1 = bf16[32,64,2880]{2,1,0:T(8,128)(2,1)} async-done(((bf16[32,64,2880]{2,1,0:T(8,128)(2,1)}), bf16[32,64,2880]{2,1,0:T(8,128)(2,1)}, u32[]{:S(2)}, u32[]{:S(2)}) %all-to-all-start.1) | async-done | bytes 11796512 | tf_op jit(solution)/shard_map/all_to_all | solution.py:183
  825.7 6.8 reduce_sum.89
  832.5 3.5 gather_fusion.1
  836.0 2.6 gather.19
  838.6 4.7 multiply_reduce_fusion
  847.6 3.5 all-to-all-start.2
  851.2 49.2 %all-gather = bf16[32,4,2880]{2,1,0:T(4,128)(2,1)} all-gather(bf16[1,4,2880]{2,1,0:T(4,128)(2,1)S(1)} %fusion.60), channel_id=1, replica_groups=mesh['dp'=4,'expert'=8] {'dp','expert'}, dimensions={0}, use_global_device_ids=true | all-gather | bytes 760320 | tf_op jit(solution)/shard_map/all_gather | solution.py:206
  904.6 4.5 fusion.79
  (102 shorter events, 34.7 us)
Async XLA Ops:
  7.2 76.5 %copy-start = (bf16[512,2880]{0,1:T(8,128)(2,1)S(1)}, bf16[512,2880]{0,1:T(8,128)(2,1)}, u32[]{:S(2)}) copy-start(bf16[512,2880]{0,1:T(8,128)(2,1)} %param.27) | copy-start | bytes 8847364
  7.2 53.2 %all-gather.4.cloned.1.call-start = ((), (), s32[]{:S(2)}) async-start(), calls=%async_computation.4 | async-start | bytes 2764800 | tf_op jit(solution)/shard_map/all_gather | solution.py:101
  7.9 108.9 %all-reduce.3.cloned.1.call-start = ((), (), s32[]{:S(2)}) async-start(), calls=%async_computation.6 | async-start | bytes 196608 | tf_op jit(solution)/shard_map/psum | solution.py:136
  62.6 6.0 copy-start.9
  62.6 6.0 copy-start.10
  79.6 3.0 copy-start.4
  81.9 0.8 copy-start.3
  83.6 81.3 %copy-start.2 = (bf16[384,720]{0,1:T(8,128)(2,1)S(1)}, bf16[384,720]{0,1:T(8,128)(2,1)}, u32[]{:S(2)}) copy-start(bf16[384,720]{0,1:T(8,128)(2,1)} %param.19) | copy-start | bytes 1658884
  83.6 81.3 %reduce-scatter.2.cloned.1.call-start = ((), (), s32[]{:S(2)}) async-start(), calls=%async_computation.5 | async-start | bytes 2764800 | tf_op jit(solution)/shard_map/reduce_scatter | solution.py:133
  87.8 79.6 %copy-start.5 = (s32[1,96,4]{1,2,0:T(4,128)S(1)}, s32[1,96,4]{1,2,0:T(4,128)}, u32[]{:S(2)}) copy-start(s32[1,96,4]{1,2,0:T(4,128)} %param.22) | copy-start | bytes 4612
  87.8 129.3 %copy-start.6 = (f32[2880]{0:T(1024)S(1)}, f32[2880]{0:T(1024)}, u32[]{:S(2)}) copy-start(f32[2880]{0:T(1024)} %param.32) | copy-start | bytes 34564
  87.8 127.2 %all-gather.6.cloned.1.call-start = ((), (), s32[]{:S(2)}) async-start(), calls=%async_computation.7 | async-start | bytes 2764800 | tf_op jit(solution)/shard_map/all_gather | solution.py:148
  554.4 4.4 copy-start.8
  554.4 271.3 %all-to-all-start.1 = ((bf16[32,64,2880]{2,1,0:T(8,128)(2,1)}), bf16[32,64,2880]{2,1,0:T(8,128)(2,1)}, u32[]{:S(2)}, u32[]{:S(2)}) async-start(bf16[32,64,2880]{2,1,0:T(8,128)(2,1)} %bitcast.114), calls=%async_computation.2 | async-start | bytes 24117248 | tf_op jit(solution)/shard_map/all_to_all | solution.py:183
  843.2 7.8 copy-start.7
  847.6 61.5 %all-to-all-start.2 = ((bf16[96,4,720]{2,0,1:T(8,128)(2,1)}), bf16[96,4,720]{2,0,1:T(8,128)(2,1)S(1)}, u32[]{:S(2)}, u32[]{:S(2)}) async-start(bf16[96,4,720]{2,0,1:T(8,128)(2,1)} %copy.68), calls=%async_computation.3 | async-start | bytes 1179648 | tf_op jit(solution)/shard_map/all_to_all | solution.py:195
  851.2 59.0 %copy-start.1 = (bf16[512,2880]{0,1:T(8,128)(2,1)S(1)}, bf16[512,2880]{0,1:T(8,128)(2,1)}, u32[]{:S(2)}) copy-start(bf16[512,2880]{0,1:T(8,128)(2,1)} %param.27) | copy-start | bytes 8847364
Sparse Core Ops, SparseCore 0:
  9.6 50.7 all-gather.3
  83.7 33.0 all-reduce.2
  119.3 45.5 reduce-scatter.1
  167.5 47.4 all-gather.5
where the time goes:
time: 918 us; the launch traced here: 917 us
  waiting for transfers between devices  435 us (47%)
  blocking collectives  316 us (34%)
  matrix products  68 us (7%)
  local copies, waits for them, and re-layouts  50.3 us (5%)
  other arithmetic  25.7 us (3%)
  between operations  14.1 us (2%)
    all_to_all x1, waiting for transfers between devices, shards(): lax.all_to_all(shares_out, ('dp', 'expert'), split_axis=0, concat_axis=0,...  267 us
    all_to_all x1, blocking collectives, shards(): lax.all_to_all(copies, ('dp', 'expert'), split_axis=0, concat_axis=0, til...  266 us
    all_gather x1, blocking collectives, shards(): spread_rows = lax.all_gather(ends, ('dp', 'expert'), axis=0, tiled=True)  49.2 us
    all_gather x1, waiting for transfers between devices, shards(): gathered_rows = lax.all_gather(hidden, 'dp', axis=1, tiled=True)  48.3 us
    reduce_scatter x1, waiting for transfers between devices, shards(): lax.psum_scatter(partial_out.astype(jnp.bfloat16), 'dp', scatter_dimensio...  48 us
    all_gather x1, waiting for transfers between devices, shards(): column_full = lax.all_gather(resid, 'dp', axis=1, tiled=True)  42.6 us
    psum x1, waiting for transfers between devices, shards(): lax.psum(jnp.dot(blended_hidden, output_down_maps, preferred_element_type...  29 us
    dot_general x1, matrix products, shards(): jnp.dot(activated, down_weight, preferred_element_type=jnp.float32)  26.6 us
  transfers between devices with their start and end apart: 6, of which 5 were waited for; matrix products, arithmetic and copies ran while one was open for 2% of the time, Pallas kernels for 0%

commit v1 on v0

--- a/solution.py
+++ b/solution.py
@@ -12,6 +12,11 @@
 theta_base = 150000.0
 adapter_scale = 2.0
 glu_alpha = 1.702
+
+
+def resolve_face(payload, mesh_dim):
+    fresh = lax.all_gather(payload, mesh_dim)
+    return jnp.sum(fresh, 0)
 
 
 def rms_scale(values, gain_row):
@@ -133,7 +138,7 @@
     mine_out = lax.psum_scatter(
         partial_out.astype(jnp.bfloat16), "dp", scatter_dimension=1, tiled=True
     ).astype(jnp.float32)
-    output_reduced = lax.psum(
+    output_reduced = resolve_face(
         jnp.dot(blended_hidden, output_down_maps, preferred_element_type=jnp.float32).astype(
             jnp.bfloat16
         ),

time: 918 us -> 888 us (0.967)
  waiting for transfers between devices: 435 us -> 389 us
  blocking collectives: 316 us -> 333 us
    psum x1 -> x0, waiting for transfers between devices: 29 us -> none  [shards(): lax.psum(jnp.dot(blended_hidden, output_down_maps, preferred_element_type...]
    reduce_scatter x1, waiting for transfers between devices: 48 us -> 29.5 us  [shards(): lax.psum_scatter(partial_out.astype(jnp.bfloat16), 'dp', scatter_dimensio...]
    all_gather x0 -> x1, blocking collectives: none -> 17.8 us  [resolve_face(): fresh = lax.all_gather(payload, mesh_dim)]
  transfers between devices with their start and end apart: 6 -> 5, of which waited for: 5 -> 4; matrix products, arithmetic and copies ran while one was open for 2% -> 2% of each run, Pallas kernels for 0% -> 0%
where the time goes in v1:
time: 888 us; the launch traced here: 887 us
  waiting for transfers between devices  389 us (44%)
  blocking collectives  333 us (38%)
  matrix products  67.3 us (8%)
  local copies, waits for them, and re-layouts  50.2 us (6%)
  other arithmetic  25.7 us (3%)
  between operations  14.1 us (2%)
    all_to_all x1, waiting for transfers between devices, shards(): lax.all_to_all(shares_out, ('dp', 'expert'), split_axis=0, concat_axis=0,...  267 us
    all_to_all x1, blocking collectives, shards(): lax.all_to_all(copies, ('dp', 'expert'), split_axis=0, concat_axis=0, til...  266 us
    all_gather x1, blocking collectives, shards(): spread_rows = lax.all_gather(ends, ('dp', 'expert'), axis=0, tiled=True)  49.2 us
    all_gather x1, waiting for transfers between devices, shards(): gathered_rows = lax.all_gather(hidden, 'dp', axis=1, tiled=True)  48.3 us
    all_gather x1, waiting for transfers between devices, shards(): column_full = lax.all_gather(resid, 'dp', axis=1, tiled=True)  43.5 us
    reduce_scatter x1, waiting for transfers between devices, shards(): lax.psum_scatter(partial_out.astype(jnp.bfloat16), 'dp', scatter_dimensio...  29.5 us
    dot_general x1, matrix products, shards(): jnp.dot(activated, down_weight, preferred_element_type=jnp.float32)  26.6 us
    all_gather x1, blocking collectives, resolve_face(): fresh = lax.all_gather(payload, mesh_dim)  17.8 us
  transfers between devices with their start and end apart: 5, of which 4 were waited for; matrix products, arithmetic and copies ran while one was open for 2% of the time, Pallas kernels for 0%

profile of v1, /device:TPU:0, one launch (start us, length us, event | category | flops | bytes accessed | tf_op | source)
XLA Modules:
  0.0 887.0 jit_solution(6553532632163200640)
XLA Ops:
  12.1 48.3 %all-gather.5.cloned.1.call-done = bf16[384,2880]{0,1:T(8,128)(2,1)} async-done(((bf16[384,720]{0,1:T(8,128)(2,1)}), bf16[384,2880]{0,1:T(8,128)(2,1)}) %all-gather.5.cloned.1.call-update) | async-done | bytes 2211856 | tf_op jit(solution)/shard_map/all_gather | solution.py:106
  62.6 5.9 fusion.11
  68.5 4.8 fusion.21
  73.3 2.5 copy.59
  82.6 3.1 convolution_convert_fusion.1
  87.1 17.8 %all-gather = bf16[1536,128]{1,0:T(8,128)(2,1)S(1)} all-gather(bf16[384,128]{1,0:T(8,128)(2,1)S(1)} %convolution_convert_fusion.2), channel_id=2, replica_groups=mesh['dp'=4,'expert'=8] {'dp'}, dimensions={0}, use_global_device_ids=true | all-gather | bytes 491520 | tf_op jit(solution)/shard_map/all_gather | solution.py:18
  105.0 29.5 %reduce-scatter.2.cloned.1.call-done = bf16[384,720]{0,1:T(8,128)(2,1)} async-done(((bf16[384,2880]{0,1:T(8,128)(2,1)}), bf16[384,720]{0,1:T(8,128)(2,1)}) %reduce-scatter.2.cloned.1.call-update) | async-done | bytes 552976 | tf_op jit(solution)/shard_map/reduce_scatter | solution.py:138
  138.8 2.9 scatter_custom_fusion
  141.8 43.5 %all-gather.7.cloned.1.call-done = bf16[384,2880]{0,1:T(8,128)(2,1)} async-done(((bf16[384,720]{0,1:T(8,128)(2,1)}), bf16[384,2880]{0,1:T(8,128)(2,1)}) %all-gather.7.cloned.1.call-update) | async-done | bytes 2211856 | tf_op jit(solution)/shard_map/all_gather | solution.py:153
  188.2 3.7 gather_fusion
  194.1 6.0 tile.8
  200.1 266.5 %all_to_all.29 = bf16[32,64,2880]{2,1,0:T(8,128)(2,1)} all-to-all(bf16[32,64,2880]{2,1,0:T(8,128)(2,1)} %bitcast.116), channel_id=1, replica_groups=mesh['dp'=4,'expert'=8] {'dp','expert'}, dimensions={0} | all-to-all | bytes 23592960 | tf_op jit(solution)/shard_map/all_to_all | solution.py:174
  466.6 15.1 %fusion.4 = f32[2048,720]{0,1:T(8,128)} fusion(bf16[2048,2880]{1,0:T(8,128)(2,1)} %bitcast.27, bf16[1,2880,720]{1,2,0:T(8,128)(2,1)} %param.34), kind=kOutput, calls=%fused_computation.15 | convolution fusion | flops 8493465600 | bytes 21841920 | tf_op jit(solution)/shard_map/dot_general | solution.py:179
  481.7 26.6 %convolution_convert_fusion = bf16[2048,2880]{0,1:T(8,128)(2,1)} fusion(bf16[1,720,2880]{2,1,0:T(8,128)(2,1)} %param.35, f32[2048,720]{0,1:T(8,128)} %fusion.4, bf16[2048,2880]{1,0:T(8,128)(2,1)} %bitcast.27, bf16[1,2880,720]{1,2,0:T(8,128)(2,1)} %param.33), kind=kOutput, calls=%fused_computation.4 | convolution fusion | flops 17004625920 | bytes 37785600 | tf_op jit(solution)/shard_map/dot_general | solution.py:184
  508.3 16.3 %copy.67 = bf16[2048,2880]{1,0:T(8,128)(2,1)} copy(bf16[2048,2880]{0,1:T(8,128)(2,1)} %convolution_convert_fusion) | data formatting | bytes 23592960 | tf_op jit(solution)/shard_map/convert_element_type | solution.py:185
  524.6 4.1 all-to-all-start.1
  529.4 266.6 %all-to-all-done.1 = bf16[32,64,2880]{2,1,0:T(8,128)(2,1)} async-done(((bf16[32,64,2880]{2,1,0:T(8,128)(2,1)}), bf16[32,64,2880]{2,1,0:T(8,128)(2,1)}, u32[]{:S(2)}, u32[]{:S(2)}) %all-to-all-start.1) | async-done | bytes 11796512 | tf_op jit(solution)/shard_map/all_to_all | solution.py:188
  796.0 6.8 reduce_sum.102
  802.9 3.5 gather_fusion.1
  806.3 2.6 gather.19
  808.9 4.7 multiply_reduce_fusion
  817.9 3.5 all-to-all-start.2
  821.5 49.2 %all-gather.1 = bf16[32,4,2880]{2,1,0:T(4,128)(2,1)} all-gather(bf16[1,4,2880]{2,1,0:T(4,128)(2,1)S(1)} %fusion.60), channel_id=1, replica_groups=mesh['dp'=4,'expert'=8] {'dp','expert'}, dimensions={0}, use_global_device_ids=true | all-gather | bytes 760320 | tf_op jit(solution)/shard_map/all_gather | solution.py:211
  875.0 4.5 fusion.79
  (99 shorter events, 35.0 us)
Async XLA Ops:
  7.2 75.4 %copy-start = (bf16[512,2880]{0,1:T(8,128)(2,1)S(1)}, bf16[512,2880]{0,1:T(8,128)(2,1)}, u32[]{:S(2)}) copy-start(bf16[512,2880]{0,1:T(8,128)(2,1)} %param.27) | copy-start | bytes 8847364
  7.2 53.2 %all-gather.5.cloned.1.call-start = ((), (), s32[]{:S(2)}) async-start(), calls=%async_computation.4 | async-start | bytes 2764800 | tf_op jit(solution)/shard_map/all_gather | solution.py:106
  7.9 126.6 %reduce-scatter.2.cloned.1.call-start = ((), (), s32[]{:S(2)}) async-start(), calls=%async_computation.5 | async-start | bytes 2764800 | tf_op jit(solution)/shard_map/reduce_scatter | solution.py:138
  62.6 6.0 copy-start.8
  62.6 6.0 copy-start.9
  81.9 0.8 copy-start.3
  82.6 51.9 %copy-start.2 = (bf16[384,720]{0,1:T(8,128)(2,1)S(1)}, bf16[384,720]{0,1:T(8,128)(2,1)}, u32[]{:S(2)}) copy-start(bf16[384,720]{0,1:T(8,128)(2,1)} %param.19) | copy-start | bytes 1658884
  85.7 51.3 %copy-start.4 = (s32[1,96,4]{1,2,0:T(4,128)S(1)}, s32[1,96,4]{1,2,0:T(4,128)}, u32[]{:S(2)}) copy-start(s32[1,96,4]{1,2,0:T(4,128)} %param.22) | copy-start | bytes 4612
  85.7 101.7 %copy-start.5 = (f32[2880]{0:T(1024)S(1)}, f32[2880]{0:T(1024)}, u32[]{:S(2)}) copy-start(f32[2880]{0:T(1024)} %param.32) | copy-start | bytes 34564
  85.7 99.6 %all-gather.7.cloned.1.call-start = ((), (), s32[]{:S(2)}) async-start(), calls=%async_computation.6 | async-start | bytes 2764800 | tf_op jit(solution)/shard_map/all_gather | solution.py:153
  524.6 4.5 copy-start.7
  524.6 271.4 %all-to-all-start.1 = ((bf16[32,64,2880]{2,1,0:T(8,128)(2,1)}), bf16[32,64,2880]{2,1,0:T(8,128)(2,1)}, u32[]{:S(2)}, u32[]{:S(2)}) async-start(bf16[32,64,2880]{2,1,0:T(8,128)(2,1)} %bitcast.115), calls=%async_computation.2 | async-start | bytes 24117248 | tf_op jit(solution)/shard_map/all_to_all | solution.py:188
  813.6 7.8 copy-start.6
  817.9 61.5 %all-to-all-start.2 = ((bf16[96,4,720]{2,0,1:T(8,128)(2,1)}), bf16[96,4,720]{2,0,1:T(8,128)(2,1)S(1)}, u32[]{:S(2)}, u32[]{:S(2)}) async-start(bf16[96,4,720]{2,0,1:T(8,128)(2,1)} %copy.68), calls=%async_computation.3 | async-start | bytes 1179648 | tf_op jit(solution)/shard_map/all_to_all | solution.py:200
  821.5 59.0 %copy-start.1 = (bf16[512,2880]{0,1:T(8,128)(2,1)S(1)}, bf16[512,2880]{0,1:T(8,128)(2,1)}, u32[]{:S(2)}) copy-start(bf16[512,2880]{0,1:T(8,128)(2,1)} %param.27) | copy-start | bytes 8847364
Sparse Core Ops, SparseCore 0:
  9.6 50.7 all-gather.4
  85.8 48.6 reduce-scatter.1
  137.1 48.1 all-gather.6
